TPU v7x, 32 devices: a whole 2x2x4 slice. The times are simulated.
32 devices in a mesh: grp: 4 (over z), emb: 8 (over y, x, core).
Axes of the slice: x: 2, y: 2, z: 4, core: 2. Of those that a mesh axis runs over, the one named last changes fastest.
Arguments:
- bottom_out: bfloat16 [4096, 128], P(('grp', 'emb')), may hold values from -6 to 6
- owner_ids: int32 [106496, 1], P(('grp', 'emb')), may hold values from 0 to 7; in each aligned block of 3328 rows (0 to 3327, 3328 to 6655, ...) at most 624 rows name the same one
- row_ids: int32 [4096, 26], P(('grp', 'emb')), may hold values from 0 to 95
- positions: int32 [4096], P(('grp', 'emb')), may hold values from 0 to 15
- labels: int32 [4096], P(('grp', 'emb')), may hold values 0 or 1
- tables: bfloat16 [26, 768, 128], P(None, 'emb'), may hold values from -6 to 6
- cross_down: bfloat16 [3456, 512], replicated, may hold values from -0.109375 to 0.109375
- cross_up: bfloat16 [512, 3456], replicated, may hold values from -0.25 to 0.25
- cross_bias: float32 [3456], replicated, may hold values from -3 to 3
- out_weight: bfloat16 [3456], replicated, may hold values from -0.109375 to 0.109375
- position_bias: float32 [16], replicated, may hold values from -2 to 2
Outputs:
- table_grad: float32 [26, 768, 128], P(None, 'emb')
- bottom_grad: bfloat16 [4096, 128], P(('grp', 'emb'))
- bias_grad: float32 [3456], replicated
Inputs may be any that keep to these rules, and one draw needn't show every extreme that they name: `owner_ids`: in every aligned block of 3328 lookups (the lookups of one device) no owner is named more than 624 times, and in some block one owner is named exactly 624 times.
All inputs are finite; a program needn't handle non-finite values. No bound on the sum of `labels` on one device may be relied on, other than what follows from the above.
Results may differ from a plain program's by a relative error of at most 0.0085.
Values may be sent and summed in bfloat16 or wider, within the bound.
No kernel may reach another device: no remote copies, remote signals or barrier semaphores. Data moves between devices by JAX's collectives and lax.ppermute only.
A program may use at most 64 MiB of HBM per device.

v0:
```python
import jax
import jax.numpy as jnp
from jax import lax
from jax.sharding import PartitionSpec as P


def local(
    bottom_out,
    owner_ids,
    row_ids,
    positions,
    labels,
    tables,
    cross_down,
    cross_up,
    cross_bias,
    out_weight,
    position_bias,
):
    sample_count, table_count = row_ids.shape
    rows_local = tables.shape[1]
    row_width = tables.shape[2]
    owner_count = lax.axis_size("emb")
    capacity = 3 * sample_count * table_count // (2 * owner_count)
    lookup_count = sample_count * table_count
    owners = owner_ids.reshape(sample_count, table_count)
    flat_owner = owners.reshape(-1)
    local_grid = jnp.arange(table_count, dtype=jnp.int32)[None, :] * rows_local + row_ids
    local_index = local_grid.reshape(-1)
    owner_marks = (flat_owner[:, None] == jnp.arange(owner_count, dtype=jnp.int32)[None, :]).astype(
        jnp.int32
    )
    ranking = jnp.cumsum(owner_marks, axis=0) - 1
    slot_index = jnp.sum(ranking * owner_marks, axis=1)
    buffer_place = flat_owner * capacity + slot_index
    flat_table = tables.reshape(table_count * rows_local, row_width)
    request = jnp.zeros((owner_count * capacity,), jnp.int32).at[buffer_place].set(local_index)
    request = request.reshape(owner_count, capacity)
    received = lax.all_to_all(request, "emb", split_axis=0, concat_axis=0, tiled=True)
    fetched = flat_table[received]
    arrived = lax.all_to_all(fetched, "emb", split_axis=0, concat_axis=0, tiled=True)
    pooled = arrived.reshape(owner_count * capacity, row_width)[buffer_place].reshape(
        sample_count, table_count * row_width
    )
    first = jnp.concatenate([bottom_out, pooled], axis=1)
    first_wide = first.astype(jnp.float32)
    weight_row = out_weight.astype(jnp.float32)
    reduced = jnp.dot(first, cross_down, preferred_element_type=jnp.float32).astype(jnp.bfloat16)
    gate_scale = jnp.dot(reduced, cross_up, preferred_element_type=jnp.float32) + cross_bias
    crossed = first_wide * gate_scale + first_wide
    position_marks = (
        positions[:, None] == jnp.arange(position_bias.shape[0], dtype=jnp.int32)[None, :]
    ).astype(jnp.float32)
    logit = jnp.sum(crossed * weight_row[None, :], axis=1) + jnp.sum(
        position_marks * position_bias[None, :], axis=1
    )
    err = jax.nn.sigmoid(logit) - labels.astype(jnp.float32)
    cotangent = err[:, None] * weight_row[None, :]
    scaled = cotangent * first_wide
    down_grad = lax.dot_general(
        scaled.astype(jnp.bfloat16),
        cross_up,
        (((1,), (1,)), ((), ())),
        preferred_element_type=jnp.float32,
    ).astype(jnp.bfloat16)
    back_term = lax.dot_general(
        down_grad, cross_down, (((1,), (1,)), ((), ())), preferred_element_type=jnp.float32
    )
    input_grad = (cotangent * (gate_scale + 1.0) + back_term).astype(jnp.bfloat16)
    bottom_grad = input_grad[:, :row_width]
    row_grads = input_grad[:, row_width:].reshape(lookup_count, row_width)
    outgoing = (
        jnp.zeros((owner_count * capacity, row_width), jnp.bfloat16).at[buffer_place].set(row_grads)
    )
    incoming = lax.all_to_all(
        outgoing.reshape(owner_count, capacity, row_width),
        "emb",
        split_axis=0,
        concat_axis=0,
        tiled=True,
    )
    local_grad = (
        jnp.zeros((table_count * rows_local, row_width), jnp.float32)
        .at[received.reshape(-1)]
        .add(incoming.reshape(owner_count * capacity, row_width).astype(jnp.float32))
    )
    summed_grad = lax.psum(local_grad.astype(jnp.bfloat16), "grp").astype(jnp.float32)
    table_grad = summed_grad.reshape(table_count, rows_local, row_width)
    bias_local = jnp.sum(scaled, axis=0)
    bias_grad = lax.psum(bias_local, ("grp", "emb"))
    return (table_grad, bottom_grad, bias_grad)


def solution(mesh):
    placed = (
        P(("grp", "emb"), None),
        P(("grp", "emb"), None),
        P(("grp", "emb"), None),
        P(("grp", "emb")),
        P(("grp", "emb")),
        P(None, "emb", None),
        P(),
        P(),
        P(),
        P(),
        P(),
    )
    return jax.shard_map(
        local,
        mesh=mesh,
        in_specs=placed,
        out_specs=(P(None, "emb", None), P(("grp", "emb"), None), P()),
        check_vma=False,
    )
```

profile of v0, /device:TPU:0, one launch (start us, length us, event | category | flops | bytes accessed | tf_op | source)
XLA Modules:
  0.0 242.6 jit_solution(920060485825970964)
XLA Ops:
  8.9 1.6 reshape.157
  11.9 5.2 %reduce-window.6 = s32[8,26,128]{2,1,0:T(8,128)} reduce-window(s32[8,26,128]{2,1,0:T(8,128)} %fusion.17, s32[]{:T(128)} %constant.10.clone.1), window={size=1x1x128 pad=0_0x0_0x127_0}, to_apply=%region_0.0 | reduce-window | flops 3381248 | bytes 212996 | tf_op jit(solution)/shard_map/reduce-window
  17.1 1.8 slice_reduce_fusion
  18.9 1.5 reduce-window.9
  22.2 13.5 %scatter_custom_fusion = s32[4992]{0:T(1024)} fusion(s32[3328]{0:T(1024)S(1)} %fusion.22, s32[3328]{0:T(1024)} %reshape.157, s32[]{:T(128)} %constant.10.clone.1), kind=kCustom, calls=%fused_computation.40 | custom fusion | bytes 20480 | tf_op jit(solution)/shard_map/scatter | solution.py:37
  37.1 9.9 %all_to_all.22 = s32[8,1,624]{2,1,0:T(1,128)S(1)} all-to-all(s32[8,1,624]{2,1,0:T(1,128)} %all_to_all.14), channel_id=1, replica_groups=mesh['grp'=4,'emb'=8] {'emb'}, dimensions={0} | all-to-all | bytes 39936 | tf_op jit(solution)/shard_map/all_to_all | solution.py:39
  51.1 12.3 %gather_fusion = bf16[4992,128]{1,0:T(8,128)(2,1)} fusion(bf16[2496,128]{1,0:T(8,128)(2,1)} %bitcast.32, s32[5120]{0:T(1024)} %pad_clamp_fusion), kind=kCustom, calls=%fused_computation | custom fusion | bytes 2575872 | tf_op jit(solution)/shard_map/gather | solution.py:40
  63.4 4.3 %all-to-all-start.1 = ((bf16[8,624,128]{2,1,0:T(8,128)(2,1)}), bf16[8,624,128]{2,1,0:T(8,128)(2,1)}, u32[]{:S(2)}, u32[]{:S(2)}) async-start(bf16[8,624,128]{2,1,0:T(8,128)(2,1)} %bitcast.34), calls=%async_computation.1 | async-start | bytes 2555904 | tf_op jit(solution)/shard_map/all_to_all | solution.py:41
  72.3 13.2 %all-to-all-done.1 = bf16[8,624,128]{2,1,0:T(8,128)(2,1)} async-done(((bf16[8,624,128]{2,1,0:T(8,128)(2,1)}), bf16[8,624,128]{2,1,0:T(8,128)(2,1)}, u32[]{:S(2)}, u32[]{:S(2)}) %all-to-all-start.1) | async-done | bytes 1277984 | tf_op jit(solution)/shard_map/all_to_all | solution.py:41
  85.5 9.2 %gather_fusion.1 = bf16[3328,128]{1,0:T(8,128)(2,1)} fusion(bf16[4992,128]{1,0:T(8,128)(2,1)} %bitcast.4, s32[4096]{0:T(1024)} %pad_clamp_fusion.1), kind=kCustom, calls=%fused_computation.1 | custom fusion | bytes 1717248 | tf_op jit(solution)/shard_map/gather | solution.py:42
  94.7 2.8 %reshape.131 = bf16[128,3328]{1,0:T(8,128)(2,1)} reshape(bf16[3328,128]{1,0:T(8,128)(2,1)} %gather_fusion.1) | data formatting | bytes 1703936 | tf_op jit(solution)/shard_map/reshape | solution.py:42
  97.5 2.1 constant_dynamic-update-slice_fusion
  99.6 5.6 %fusion.6 = (f32[128]{0:T(128)}, f32[128,3456]{1,0:T(8,128)}) fusion(bf16[128,3456]{1,0:T(8,128)(2,1)} %constant_dynamic-update-slice_fusion, f32[3456]{0:T(1024)S(1)} %convert_element_type.40, f32[3456]{0:T(1024)} %param.19, bf16[512,3456]{1,0:T(8,128)(2,1)} %param.18, bf16[3456,512]{1,0:T(8,128)(2,1)S(1)} %copy-done), kind=kOutput, calls=%fused_computation.16 | convolution fusion | flops 908689280 | bytes 9760256 | tf_op jit(solution)/shard_map/dot_general | solution.py:49
  106.4 6.1 %fusion = bf16[128,3456]{1,0:T(8,128)(2,1)} fusion(bf16[3456,512]{1,0:T(8,128)(2,1)S(1)} %copy-done, f32[128,3456]{1,0:T(8,128)} %get-tuple-element.4, bf16[512,3456]{1,0:T(8,128)(2,1)} %param.18, bf16[128,3456]{1,0:T(8,128)(2,1)} %constant_dynamic-update-slice_fusion, f32[128]{0:T(128)} %divide_subtract_fusion, f32[3456]{0:T(1024)S(1)} %convert_element_type.40), kind=kOutput, calls=%fused_computation.7 | convolution fusion | flops 910016512 | bytes 10631168 | tf_op jit(solution)/shard_map/dot_general | solution.py:66
  112.4 2.1 slice.21
  114.5 2.9 %reshape.165 = bf16[3328,128]{1,0:T(8,128)(2,1)} reshape(bf16[128,3328]{1,0:T(8,128)(2,1)} %slice.21) | data formatting | bytes 1703936 | tf_op jit(solution)/shard_map/reshape | solution.py:71
  117.4 14.9 %scatter_custom_fusion.1 = bf16[4992,128]{1,0:T(8,128)(2,1)} fusion(s32[3328]{0:T(1024)} %copy-done.2, bf16[3328,128]{1,0:T(8,128)(2,1)} %reshape.165, bf16[]{:T(256)} %constant.5.clone.1), kind=kCustom, calls=%fused_computation.21 | custom fusion | bytes 1278464 | tf_op jit(solution)/shard_map/scatter | solution.py:73
  132.3 4.3 %all-to-all-start.2 = ((bf16[8,624,128]{2,1,0:T(8,128)(2,1)}), bf16[8,624,128]{2,1,0:T(8,128)(2,1)}, u32[]{:S(2)}, u32[]{:S(2)}) async-start(bf16[8,624,128]{2,1,0:T(8,128)(2,1)} %bitcast.33), calls=%async_computation.2 | async-start | bytes 2555904 | tf_op jit(solution)/shard_map/all_to_all | solution.py:75
  141.0 13.4 %all-to-all-done.2 = bf16[8,624,128]{2,1,0:T(8,128)(2,1)} async-done(((bf16[8,624,128]{2,1,0:T(8,128)(2,1)}), bf16[8,624,128]{2,1,0:T(8,128)(2,1)}, u32[]{:S(2)}, u32[]{:S(2)}) %all-to-all-start.2) | async-done | bytes 1277984 | tf_op jit(solution)/shard_map/all_to_all | solution.py:75
  154.4 33.9 %scatter_custom_fusion.2 = f32[2496,128]{1,0:T(8,128)} fusion(s32[4992]{0:T(1024)} %fusion.21, bf16[4992,128]{1,0:T(8,128)(2,1)} %bitcast.8, f32[]{:T(128)} %constant.9.clone.1), kind=kCustom, calls=%fused_computation.9 | custom fusion | flops 1277952 | bytes 2556416 | tf_op jit(solution)/shard_map/scatter-add | solution.py:85
  188.4 2.2 convert_element_type.47
  192.0 2.1 fusion.3
  194.1 39.5 %psum.15 = f32[3456]{0:T(1024)} all-reduce(f32[3456]{0:T(1024)} %fusion.3), channel_id=1, replica_groups=mesh['grp'=4,'emb'=8] {'grp','emb'}, use_global_device_ids=true, to_apply=%region_10.11 | all-reduce | flops 3456 | bytes 27648 | tf_op jit(solution)/shard_map/psum | solution.py:90
  233.5 2.3 reshape.135
  (30 shorter events, 22.1 us)
Async XLA Ops:
  7.2 92.5 %copy-start = (bf16[3456,512]{1,0:T(8,128)(2,1)S(1)}, bf16[3456,512]{1,0:T(8,128)(2,1)}, u32[]{:S(2)}) copy-start(bf16[3456,512]{1,0:T(8,128)(2,1)} %param.17) | copy-start | bytes 10616836
  22.2 41.2 %copy-start.2 = (s32[3328]{0:T(1024)}, s32[3328]{0:T(1024)S(1)}, u32[]{:S(2)}) copy-start(s32[3328]{0:T(1024)S(1)} %fusion.22) | copy-start | bytes 39940
  47.1 0.6 copy-start.1
  63.4 22.1 %all-to-all-start.1 = ((bf16[8,624,128]{2,1,0:T(8,128)(2,1)}), bf16[8,624,128]{2,1,0:T(8,128)(2,1)}, u32[]{:S(2)}, u32[]{:S(2)}) async-start(bf16[8,624,128]{2,1,0:T(8,128)(2,1)} %bitcast.34), calls=%async_computation.1 | async-start | bytes 2555904 | tf_op jit(solution)/shard_map/all_to_all | solution.py:41
  132.3 22.1 %all-to-all-start.2 = ((bf16[8,624,128]{2,1,0:T(8,128)(2,1)}), bf16[8,624,128]{2,1,0:T(8,128)(2,1)}, u32[]{:S(2)}, u32[]{:S(2)}) async-start(bf16[8,624,128]{2,1,0:T(8,128)(2,1)} %bitcast.33), calls=%async_computation.2 | async-start | bytes 2555904 | tf_op jit(solution)/shard_map/all_to_all | solution.py:75
  136.5 97.0 %all-reduce.2.cloned.1.call-start = ((), (), s32[]{:S(2)}) async-start(), calls=%async_computation.3 | async-start | bytes 1277952 | tf_op jit(solution)/shard_map/psum | solution.py:87
Sparse Core Ops, SparseCore 0:
  190.7 39.9 all-reduce.1
where the time goes:
time: 245 us; the launch traced here: 243 us
  local copies, waits for them, and re-layouts  71.5 us (29%)
  other arithmetic  60.6 us (25%)
  blocking collectives  49.4 us (20%)
  waiting for transfers between devices  26.7 us (11%)
  between operations  14.1 us (6%)
  matrix products  11.6 us (5%)
  starting transfers between devices  8.73 us (4%)
    psum x1, blocking collectives, local(): bias_grad = lax.psum(bias_local, ('grp', 'emb'))  39.5 us
    scatter-add x1, other arithmetic, local(): local_grad = jnp.zeros((table_count * rows_local, row_width), jnp.float32...  33.9 us
    scatter x1, local copies, waits for them, and re-layouts, local(): jnp.zeros((owner_count * capacity, row_width), jnp.bfloat16)  14.9 us
    scatter x1, local copies, waits for them, and re-layouts, local(): jnp.zeros((owner_count * capacity,), jnp.int32).at[buffer_place]  13.5 us
    all_to_all x1, waiting for transfers between devices, local(): lax.all_to_all(outgoing.reshape(owner_count, capacity, row_width), 'emb',...  13.4 us
    all_to_all x1, waiting for transfers between devices, local(): lax.all_to_all(fetched, 'emb', split_axis=0, concat_axis=0, tiled=True)  13.2 us
    gather x1, local copies, waits for them, and re-layouts, local(): fetched = flat_table[received]  12.3 us
    all_to_all x1, blocking collectives, local(): lax.all_to_all(request, 'emb', split_axis=0, concat_axis=0, tiled=True)  9.94 us
  transfers between devices with their start and end apart: 3, of which 2 were waited for; matrix products, arithmetic and copies ran while one was open for 5% of the time, Pallas kernels for 0%

commit v1 on v0

--- a/solution.py
+++ b/solution.py
@@ -2,6 +2,17 @@
 import jax.numpy as jnp
 from jax import lax
 from jax.sharding import PartitionSpec as P
+
+
+def split_up(array, dim, size):
+    before, after = (array.shape[:dim], array.shape[dim + 1 :])
+    return jnp.moveaxis(array.reshape(*before, size, -1, *after), dim, 0)
+
+
+def joined_along(blocks, dim):
+    blocks = jnp.moveaxis(blocks, 0, dim)
+    shape = blocks.shape
+    return blocks.reshape(*shape[:dim], shape[dim] * shape[dim + 1], *shape[dim + 2 :])
 
 
 def local(
@@ -38,7 +49,15 @@
     request = request.reshape(owner_count, capacity)
     received = lax.all_to_all(request, "emb", split_axis=0, concat_axis=0, tiled=True)
     fetched = flat_table[received]
-    arrived = lax.all_to_all(fetched, "emb", split_axis=0, concat_axis=0, tiled=True)
+    length, index = (lax.axis_size("emb"), lax.axis_index("emb"))
+    pieces = split_up(fetched, 0, length)
+    filled = pieces
+    for turn in range(1, length):
+        target, source = ((index + turn) % length, (index - turn) % length)
+        sent = lax.dynamic_index_in_dim(pieces, target, 0)
+        other = lax.ppermute(sent, "emb", [(i, (i + turn) % length) for i in range(length)])
+        filled = lax.dynamic_update_slice_in_dim(filled, other, source, axis=0)
+    arrived = joined_along(filled, 0)
     pooled = arrived.reshape(owner_count * capacity, row_width)[buffer_place].reshape(
         sample_count, table_count * row_width
     )

time: 245 us -> 248 us (1.012)
  blocking collectives: 49.4 us -> 39.5 us
  starting transfers between devices: 8.73 us -> 18.1 us
  local copies, waits for them, and re-layouts: 71.5 us -> 79.7 us
  waiting for transfers between devices: 26.7 us -> 20.7 us
    all_to_all x1 -> x0, blocking collectives: 9.94 us -> none  [local(): lax.all_to_all(request, 'emb', split_axis=0, concat_axis=0, tiled=True)]
    all_to_all x1, waiting for transfers between devices: 13.2 us -> 3.6 us  [local(): lax.all_to_all(request, 'emb', split_axis=0, concat_axis=0, tiled=True)]
    dynamic_update_slice x0 -> x7, local copies, waits for them, and re-layouts: none -> 6.55 us  [local(): filled = lax.dynamic_update_slice_in_dim(filled, other, source, axis=0)]
    ppermute x0 -> x7, starting transfers between devices: none -> 6.38 us  [local(): lax.ppermute(sent, 'emb', [(i, (i + turn) % length) for i in range(length)])]
    ppermute x0 -> x7, waiting for transfers between devices: none -> 3.12 us  [local(): lax.ppermute(sent, 'emb', [(i, (i + turn) % length) for i in range(length)])]
  transfers between devices with their start and end apart: 3 -> 10, of which waited for: 2 -> 5; matrix products, arithmetic and copies ran while one was open for 5% -> 7% of each run, Pallas kernels for 0% -> 0%
where the time goes in v1:
time: 248 us; the launch traced here: 246 us
  local copies, waits for them, and re-layouts  79.7 us (32%)
  other arithmetic  61.9 us (25%)
  blocking collectives  39.5 us (16%)
  waiting for transfers between devices  20.7 us (8%)
  starting transfers between devices  18.1 us (7%)
  between operations  14.1 us (6%)
  matrix products  11.6 us (5%)
    psum x1, blocking collectives, local(): bias_grad = lax.psum(bias_local, ('grp', 'emb'))  39.5 us
    scatter-add x1, other arithmetic, local(): local_grad = jnp.zeros((table_count * rows_local, row_width), jnp.float32...  33.9 us
    scatter x1, local copies, waits for them, and re-layouts, local(): jnp.zeros((owner_count * capacity, row_width), jnp.bfloat16)  14.9 us
    all_to_all x1, waiting for transfers between devices, local(): lax.all_to_all(outgoing.reshape(owner_count, capacity, row_width), 'emb',...  13.9 us
    scatter x1, local copies, waits for them, and re-layouts, local(): jnp.zeros((owner_count * capacity,), jnp.int32).at[buffer_place]  13.5 us
    gather x1, local copies, waits for them, and re-layouts, local(): fetched = flat_table[received]  12.3 us
    gather x1, local copies, waits for them, and re-layouts, local(): arrived.reshape(owner_count * capacity, row_width)[buffer_place]  9.15 us
    another operation x2, other arithmetic  6.68 us
  transfers between devices with their start and end apart: 10, of which 5 were waited for; matrix products, arithmetic and copies ran while one was open for 7% of the time, Pallas kernels for 0%

profile of v1, /device:TPU:0, one launch (start us, length us, event | category | flops | bytes accessed | tf_op | source)
XLA Modules:
  0.0 245.5 jit_solution(3279798971399338717)
XLA Ops:
  9.4 5.2 %reduce-window.6 = s32[8,26,128]{2,1,0:T(8,128)} reduce-window(s32[8,26,128]{2,1,0:T(8,128)} %fusion.17, s32[]{:T(128)} %constant.117.clone.1), window={size=1x1x128 pad=0_0x0_0x127_0}, to_apply=%region_0.0 | reduce-window | flops 3381248 | bytes 212996 | tf_op jit(solution)/shard_map/reduce-window
  14.6 1.8 slice_reduce_fusion
  24.1 13.5 %scatter_custom_fusion = s32[4992]{0:T(1024)} fusion(s32[3328]{0:T(1024)S(1)} %fusion.22, s32[3328]{0:T(1024)} %reshape.164, s32[]{:T(128)} %constant.117.clone.1), kind=kCustom, calls=%fused_computation.47 | custom fusion | bytes 20480 | tf_op jit(solution)/shard_map/scatter | solution.py:48
  39.0 5.2 %all-to-all-start = ((s32[8,1,624]{2,1,0:T(1,128)}), s32[8,1,624]{2,1,0:T(1,128)}, u32[]{:S(2)}, u32[]{:S(2)}) async-start(s32[8,1,624]{2,1,0:T(1,128)} %all_to_all.11), calls=%async_computation | async-start | bytes 40960 | tf_op jit(solution)/shard_map/all_to_all | solution.py:50
  45.5 3.6 %all-to-all-done = s32[8,1,624]{2,1,0:T(1,128)} async-done(((s32[8,1,624]{2,1,0:T(1,128)}), s32[8,1,624]{2,1,0:T(1,128)}, u32[]{:S(2)}, u32[]{:S(2)}) %all-to-all-start) | async-done | bytes 20000 | tf_op jit(solution)/shard_map/all_to_all | solution.py:50
  53.2 12.3 %gather_fusion = bf16[4992,128]{1,0:T(8,128)(2,1)} fusion(bf16[2496,128]{1,0:T(8,128)(2,1)} %bitcast.45, s32[5120]{0:T(1024)} %pad_clamp_fusion), kind=kCustom, calls=%fused_computation | custom fusion | bytes 2575872 | tf_op jit(solution)/shard_map/gather | solution.py:51
  65.5 2.3 dynamic-slice_bitcast_fusion
  75.7 1.6 constant_dynamic-update-slice_fusion.8
  80.3 1.8 collective-permute-done.2
  85.9 9.2 %gather_fusion.1 = bf16[3328,128]{1,0:T(8,128)(2,1)} fusion(bf16[4992,128]{1,0:T(8,128)(2,1)} %bitcast.48, s32[4096]{0:T(1024)} %pad_clamp_fusion.1), kind=kCustom, calls=%fused_computation.1 | custom fusion | bytes 1717248 | tf_op jit(solution)/shard_map/gather | solution.py:61
  95.0 2.8 %reshape.138 = bf16[128,3328]{1,0:T(8,128)(2,1)} reshape(bf16[3328,128]{1,0:T(8,128)(2,1)} %gather_fusion.1) | data formatting | bytes 1703936 | tf_op jit(solution)/shard_map/reshape | solution.py:61
  97.8 2.1 constant_dynamic-update-slice_fusion
  99.9 5.6 %fusion.6 = (f32[128]{0:T(128)}, f32[128,3456]{1,0:T(8,128)}) fusion(bf16[128,3456]{1,0:T(8,128)(2,1)} %constant_dynamic-update-slice_fusion, f32[3456]{0:T(1024)S(1)} %convert_element_type.40, f32[3456]{0:T(1024)} %param.19, bf16[512,3456]{1,0:T(8,128)(2,1)} %param.18, bf16[3456,512]{1,0:T(8,128)(2,1)S(1)} %copy-done), kind=kOutput, calls=%fused_computation.16 | convolution fusion | flops 908689280 | bytes 9760256 | tf_op jit(solution)/shard_map/dot_general | solution.py:68
  106.7 6.1 %fusion = bf16[128,3456]{1,0:T(8,128)(2,1)} fusion(bf16[3456,512]{1,0:T(8,128)(2,1)S(1)} %copy-done, f32[128,3456]{1,0:T(8,128)} %get-tuple-element.11, bf16[512,3456]{1,0:T(8,128)(2,1)} %param.18, bf16[128,3456]{1,0:T(8,128)(2,1)} %constant_dynamic-update-slice_fusion, f32[128]{0:T(128)} %divide_subtract_fusion, f32[3456]{0:T(1024)S(1)} %convert_element_type.40), kind=kOutput, calls=%fused_computation.7 | convolution fusion | flops 910016512 | bytes 10631168 | tf_op jit(solution)/shard_map/dot_general | solution.py:85
  112.8 2.1 slice.21
  114.9 2.9 %reshape.172 = bf16[3328,128]{1,0:T(8,128)(2,1)} reshape(bf16[128,3328]{1,0:T(8,128)(2,1)} %slice.21) | data formatting | bytes 1703936 | tf_op jit(solution)/shard_map/reshape | solution.py:90
  117.8 14.9 %scatter_custom_fusion.1 = bf16[4992,128]{1,0:T(8,128)(2,1)} fusion(s32[3328]{0:T(1024)} %copy-done.1, bf16[3328,128]{1,0:T(8,128)(2,1)} %reshape.172, bf16[]{:T(256)} %constant.123.clone.1), kind=kCustom, calls=%fused_computation.21 | custom fusion | bytes 1278464 | tf_op jit(solution)/shard_map/scatter | solution.py:92
  132.6 6.5 %all-to-all-start.1 = ((bf16[8,624,128]{2,1,0:T(8,128)(2,1)}), bf16[8,624,128]{2,1,0:T(8,128)(2,1)}, u32[]{:S(2)}, u32[]{:S(2)}) async-start(bf16[8,624,128]{2,1,0:T(8,128)(2,1)} %bitcast.49), calls=%async_computation.1 | async-start | bytes 2555904 | tf_op jit(solution)/shard_map/all_to_all | solution.py:94
  143.4 13.9 %all-to-all-done.1 = bf16[8,624,128]{2,1,0:T(8,128)(2,1)} async-done(((bf16[8,624,128]{2,1,0:T(8,128)(2,1)}), bf16[8,624,128]{2,1,0:T(8,128)(2,1)}, u32[]{:S(2)}, u32[]{:S(2)}) %all-to-all-start.1) | async-done | bytes 1277984 | tf_op jit(solution)/shard_map/all_to_all | solution.py:94
  157.3 33.9 %scatter_custom_fusion.2 = f32[2496,128]{1,0:T(8,128)} fusion(s32[4992]{0:T(1024)} %fusion.21, bf16[4992,128]{1,0:T(8,128)(2,1)} %bitcast.16, f32[]{:T(128)} %constant.116.clone.1), kind=kCustom, calls=%fused_computation.9 | custom fusion | flops 1277952 | bytes 2556416 | tf_op jit(solution)/shard_map/scatter-add | solution.py:104
  191.2 2.2 convert_element_type.47
  194.8 2.1 fusion.3
  196.9 39.5 %psum.15 = f32[3456]{0:T(1024)} all-reduce(f32[3456]{0:T(1024)} %fusion.3), channel_id=1, replica_groups=mesh['grp'=4,'emb'=8] {'grp','emb'}, use_global_device_ids=true, to_apply=%region_10.11 | all-reduce | flops 3456 | bytes 27648 | tf_op jit(solution)/shard_map/psum | solution.py:109
  236.4 2.3 reshape.142
  (51 shorter events, 38.2 us)
Async XLA Ops:
  7.2 92.8 %copy-start = (bf16[3456,512]{1,0:T(8,128)(2,1)S(1)}, bf16[3456,512]{1,0:T(8,128)(2,1)}, u32[]{:S(2)}) copy-start(bf16[3456,512]{1,0:T(8,128)(2,1)} %param.17) | copy-start | bytes 10616836
  19.7 49.4 %copy-start.1 = (s32[3328]{0:T(1024)}, s32[3328]{0:T(1024)S(1)}, u32[]{:S(2)}) copy-start(s32[3328]{0:T(1024)S(1)} %fusion.22) | copy-start | bytes 39940
  39.0 10.1 %all-to-all-start = ((s32[8,1,624]{2,1,0:T(1,128)}), s32[8,1,624]{2,1,0:T(1,128)}, u32[]{:S(2)}, u32[]{:S(2)}) async-start(s32[8,1,624]{2,1,0:T(1,128)} %all_to_all.11), calls=%async_computation | async-start | bytes 40960 | tf_op jit(solution)/shard_map/all_to_all | solution.py:50
  65.5 2.3 copy-start.2
  67.9 6.4 %collective-permute-start = (bf16[1,1,624,128]{3,2,0,1:T(8,128)(2,1)}, bf16[1,1,624,128]{3,2,0,1:T(8,128)(2,1)}, u32[]{:S(2)}, u32[]{:S(2)}) collective-permute-start(bf16[1,1,624,128]{3,2,0,1:T(8,128)(2,1)} %get-tuple-element.8), channel_id=1, source_target_pairs={{0,1},{1,2},{2,3},{3,4},{4,5},{5,6},{6,7},{7,0},{8,9},{9,10},{10,1... | collective-permute-start | bytes 479240 | tf_op jit(solution)/shard_map/ppermute | solution.py:58
  68.5 8.8 %collective-permute-start.1 = (bf16[1,1,624,128]{3,2,0,1:T(8,128)(2,1)}, bf16[1,1,624,128]{3,2,0,1:T(8,128)(2,1)}, u32[]{:S(2)}, u32[]{:S(2)}) collective-permute-start(bf16[1,1,624,128]{3,2,0,1:T(8,128)(2,1)} %get-tuple-element.7), channel_id=1, source_target_pairs={{0,2},{1,3},{2,4},{3,5},{4,6},{5,7},{6,0},{7,1},{8,10},{9,11},{10,... | collective-permute-start | bytes 479240 | tf_op jit(solution)/shard_map/ppermute | solution.py:58
  70.4 11.7 %collective-permute-start.2 = (bf16[1,1,624,128]{3,2,0,1:T(8,128)(2,1)}, bf16[1,1,624,128]{3,2,0,1:T(8,128)(2,1)S(1)}, u32[]{:S(2)}, u32[]{:S(2)}) collective-permute-start(bf16[1,1,624,128]{3,2,0,1:T(8,128)(2,1)} %get-tuple-element.6), channel_id=1, source_target_pairs={{0,3},{1,4},{2,5},{3,6},{4,7},{5,0},{6,1},{7,2},{8,11},{9,12},{10,... | collective-permute-start | bytes 479240 | tf_op jit(solution)/shard_map/ppermute | solution.py:58
  71.8 11.0 %collective-permute-start.3 = (bf16[1,1,624,128]{3,2,0,1:T(8,128)(2,1)}, bf16[1,1,624,128]{3,2,0,1:T(8,128)(2,1)S(1)}, u32[]{:S(2)}, u32[]{:S(2)}) collective-permute-start(bf16[1,1,624,128]{3,2,0,1:T(8,128)(2,1)} %get-tuple-element.5), channel_id=1, source_target_pairs={{0,4},{1,5},{2,6},{3,7},{4,0},{5,1},{6,2},{7,3},{8,12},{9,13},{10,... | collective-permute-start | bytes 479240 | tf_op jit(solution)/shard_map/ppermute | solution.py:58
  73.3 10.5 %collective-permute-start.4 = (bf16[1,1,624,128]{3,2,0,1:T(8,128)(2,1)}, bf16[1,1,624,128]{3,2,0,1:T(8,128)(2,1)S(1)}, u32[]{:S(2)}, u32[]{:S(2)}) collective-permute-start(bf16[1,1,624,128]{3,2,0,1:T(8,128)(2,1)} %get-tuple-element.4), channel_id=1, source_target_pairs={{0,5},{1,6},{2,7},{3,0},{4,1},{5,2},{6,3},{7,4},{8,13},{9,14},{10,... | collective-permute-start | bytes 479240 | tf_op jit(solution)/shard_map/ppermute | solution.py:58
  74.2 10.3 %collective-permute-start.5 = (bf16[1,1,624,128]{3,2,0,1:T(8,128)(2,1)}, bf16[1,1,624,128]{3,2,0,1:T(8,128)(2,1)S(1)}, u32[]{:S(2)}, u32[]{:S(2)}) collective-permute-start(bf16[1,1,624,128]{3,2,0,1:T(8,128)(2,1)} %get-tuple-element.9), channel_id=1, source_target_pairs={{0,6},{1,7},{2,0},{3,1},{4,2},{5,3},{6,4},{7,5},{8,14},{9,15},{10,... | collective-permute-start | bytes 479240 | tf_op jit(solution)/shard_map/ppermute | solution.py:58
  77.3 7.9 %collective-permute-start.6 = (bf16[1,1,624,128]{3,2,0,1:T(8,128)(2,1)}, bf16[1,1,624,128]{3,2,0,1:T(8,128)(2,1)S(1)}, u32[]{:S(2)}, u32[]{:S(2)}) collective-permute-start(bf16[1,1,624,128]{3,2,0,1:T(8,128)(2,1)} %get-tuple-element.3), channel_id=1, source_target_pairs={{0,7},{1,0},{2,1},{3,2},{4,3},{5,4},{6,5},{7,6},{8,15},{9,8},{10,9... | collective-permute-start | bytes 479240 | tf_op jit(solution)/shard_map/ppermute | solution.py:58
  132.6 24.7 %all-to-all-start.1 = ((bf16[8,624,128]{2,1,0:T(8,128)(2,1)}), bf16[8,624,128]{2,1,0:T(8,128)(2,1)}, u32[]{:S(2)}, u32[]{:S(2)}) async-start(bf16[8,624,128]{2,1,0:T(8,128)(2,1)} %bitcast.49), calls=%async_computation.1 | async-start | bytes 2555904 | tf_op jit(solution)/shard_map/all_to_all | solution.py:94
  139.1 97.3 %all-reduce.2.cloned.1.call-start = ((), (), s32[]{:S(2)}) async-start(), calls=%async_computation.2 | async-start | bytes 1277952 | tf_op jit(solution)/shard_map/psum | solution.py:106
Sparse Core Ops, SparseCore 0:
  193.6 39.9 all-reduce.1
